TPU v7x, 32 devices: a whole 2x2x4 slice. The times are simulated.
32 devices in a mesh: group: 2 (over x), span: 16 (over z, y, core).
Axes of the slice: x: 2, y: 2, z: 4, core: 2. Of those that a mesh axis runs over, the one named last changes fastest.
Arguments:
- queries: bfloat16 [8192, 2560], P(('group', 'span')), parts along dimension 0, may hold values from -6 to 6
- keys_values: bfloat16 [2, 8192, 2560], P(None, ('group', 'span')), parts along dimension 1, may hold values from -6 to 6
- owner: int32 [2], P('group'), parts along dimension 0, may hold values from 0 to 15
- span_mask: int32 [32, 3], P('group'), parts along dimension 0, may hold values 0 or 1
- lengths: int32 [32], P('group'), parts along dimension 0, may hold values from 128 to 256, as said below
- frames: bfloat16 [6, 16, 52, 384], P('group', 'span'), parts along dimension 0, may hold values from -6 to 6
- past_frames: bfloat16 [4, 16, 52, 384], P('group', 'span'), parts along dimension 0, may hold values from -5 to 5
- norm_gain: float32 [384], replicated, may hold values from 0.5 to 1.5
- conv_weight: bfloat16 [3, 3, 3, 384, 384], replicated, may hold values from -0.0625 to 0.0625
- conv_bias: float32 [384], replicated, may hold values from -3 to 3
Outputs:
- attended: bfloat16 [8192, 2560], P(('group', 'span')), parts along dimension 0
- decoded: bfloat16 [6, 16, 52, 384], P('group', 'span'), parts along dimension 0
There are 2 independent parts, one for each index of `group`. A program takes and returns all parts, laid end to end along the dimension named above; an argument that names none is the same for every part. Nothing has to cross between parts.
Inputs may be any that keep to these rules, and one draw needn't show every extreme that they name: `lengths`: at least one slot holds exactly 256 tokens.
All inputs are finite; a program needn't handle non-finite values.
Results may differ from a plain program's by a relative error of at most 0.005.
Values may be sent and summed in bfloat16 or wider, within the bound.
No kernel may reach another device: no remote copies, remote signals or barrier semaphores. Data moves between devices by JAX's collectives and lax.ppermute only.
A program may use at most 128 MiB of HBM per device.

v0:
```python
import jax
import jax.numpy as jnp
from jax import lax
from jax.sharding import PartitionSpec as P

H = 20
DH = 128
WIN = 4
HG = 10


def spread(block, axis, source):
    block = jnp.where(lax.axis_index(axis) == source, block, jnp.zeros_like(block))
    return lax.psum(block, axis)


def extended_2(block, sides, width):
    for axis, dim in sides:
        count = lax.axis_size(axis)
        forward = [(i, i + 1) for i in range(count - 1)]
        backward = [(target, source) for source, target in forward]
        low = lax.ppermute(
            lax.slice_in_dim(block, block.shape[dim] - width, None, axis=dim), axis, forward
        )
        high = lax.ppermute(lax.slice_in_dim(block, 0, width, axis=dim), axis, backward)
        block = jnp.concatenate([low, block, high], axis=dim)
    return block


def move(value, pairs):
    return lax.ppermute(value, "span", pairs)


def window_blocks(kv, devices):
    rows = devices // 4
    lane = lax.axis_index("span") % 4

    def at(r, l):
        return 4 * (r % rows) + l

    rng = range(rows)
    rail1 = move(kv, [(at(r, 3), at(r + 1, 2)) for r in rng])
    rail0 = move(kv, [(at(r, 1), at(r + 1, 0)) for r in rng])
    y_up = move(kv, [(at(r, 0), at(r, 2)) for r in rng] + [(at(r, 1), at(r, 3)) for r in rng])
    y_down = move(kv, [(at(r, 2), at(r, 1)) for r in rng])
    chip = move(kv, [(at(r, 0), at(r, 1)) for r in rng] + [(at(r, 2), at(r, 3)) for r in rng])
    swap = move(y_up, [(at(r, 3), at(r, 2)) for r in rng] + [(at(r, 2), at(r, 3)) for r in rng])
    down2 = move(rail1, [(at(r, 2), at(r, 0)) for r in rng])
    rail0b = move(y_down, [(at(r, 1), at(r + 1, 0)) for r in rng])
    pair = move(jnp.stack([down2, rail0b]), [(at(r, 0), at(r, 1)) for r in rng])

    def pick(*options):
        out = options[0]
        for l in range(1, 4):
            out = jnp.where(lane == l, options[l], out)
        return out

    b1 = pick(down2, chip, swap, chip)
    b2 = pick(rail0b, pair[0], y_up, y_up)
    b3 = pick(rail0, pair[1], rail1, swap)
    return (b1, b2, b3)


def part_stats(q, k, valid, scale):
    scores = jnp.einsum("qhd,khd->hqk", q, k, preferred_element_type=jnp.float32) * scale
    return jnp.where(valid[None, None, :], scores, -jnp.inf)


def shards(
    queries,
    keys_values,
    owner,
    span_mask,
    lengths,
    frames,
    past_frames,
    norm_gain,
    conv_weight,
    conv_bias,
):
    devices = lax.axis_size("span")
    place = lax.axis_index("span")
    anchor = owner[0]
    position = (place - anchor - 1) % devices
    tok_rows = queries.shape[0]
    row_ids = jnp.arange(tok_rows, dtype=jnp.int32)
    anchor_k = spread(keys_values[0], "span", anchor)
    later_v, anchor_k = lax.optimization_barrier((keys_values[1], anchor_k))
    anchor_v = spread(later_v, "span", anchor)
    b1, b2, b3 = window_blocks(keys_values, devices)
    blocks = [keys_values, b1, b2, b3]
    valid_list = [row_ids < lengths[place]]
    for offset in range(1, WIN):
        source = (place - offset) % devices
        allowed = (position >= offset) & (span_mask[position, offset - 1] == 1)
        valid_list.append(allowed & (row_ids < lengths[source]))
    anchor_valid = (place != anchor) & (row_ids < lengths[anchor])
    window_kv = jnp.concatenate(blocks, axis=1)
    window_valid = jnp.concatenate(valid_list)
    score_scale = DH ** (-0.5)
    partial = []
    for head_block in range(H // HG):
        first_col = head_block * HG * DH
        last_col = first_col + HG * DH
        q = queries[:, first_col:last_col].reshape(tok_rows, HG, DH)
        wk = window_kv[0, :, first_col:last_col].reshape(-1, HG, DH)
        wv = window_kv[1, :, first_col:last_col].reshape(-1, HG, DH)
        ak = anchor_k[:, first_col:last_col].reshape(-1, HG, DH)
        ws = part_stats(q, wk, window_valid, score_scale)
        a_s = part_stats(q, ak, anchor_valid, score_scale)
        top = jnp.maximum(jnp.max(ws, axis=-1, keepdims=True), jnp.max(a_s, axis=-1, keepdims=True))
        w_exp = jnp.exp(ws - top)
        a_exp = jnp.exp(a_s - top)
        total = jnp.sum(w_exp, axis=-1, keepdims=True) + jnp.sum(a_exp, axis=-1, keepdims=True)
        w_probs = (w_exp / total).astype(jnp.bfloat16)
        a_probs = (a_exp / total).astype(jnp.bfloat16)
        w_out = jnp.einsum("hqk,khd->hqd", w_probs, wv, preferred_element_type=jnp.float32)
        partial.append((w_out, a_probs))
    anchor_v, partial = lax.optimization_barrier((anchor_v, partial))
    pieces = []
    for head_block, (w_out, a_probs) in enumerate(partial):
        first_col = head_block * HG * DH
        last_col = first_col + HG * DH
        av = anchor_v[:, first_col:last_col].reshape(-1, HG, DH)
        blended = w_out + jnp.einsum(
            "hqk,khd->hqd", a_probs, av, preferred_element_type=jnp.float32
        )
        pieces.append(jnp.transpose(blended, (1, 0, 2)).reshape(tok_rows, HG * DH))
    attended = jnp.concatenate(pieces, axis=1)
    attended = jnp.where(row_ids[:, None] < lengths[place], attended, 0.0).astype(jnp.bfloat16)
    features = frames.astype(jnp.float32)
    squares = jnp.mean(features * features, axis=-1, keepdims=True)
    normed = features * lax.rsqrt(squares + 1e-06) * norm_gain
    activated = jax.nn.silu(normed).astype(jnp.bfloat16)
    stacked = jnp.concatenate([past_frames, activated], axis=0)
    extended = extended_2(stacked, (("span", 1),), 1)
    padded = jnp.pad(extended, ((0, 0), (0, 0), (1, 1), (0, 0)))
    frame_count = frames.shape[0]
    rows_here = frames.shape[1]
    col_count = frames.shape[2]
    channels = frames.shape[3]
    windows = []
    for frame_tap in range(3):
        for row_tap in range(3):
            for col_tap in range(3):
                windows.append(
                    padded[
                        frame_tap : frame_tap + frame_count,
                        row_tap : row_tap + rows_here,
                        col_tap : col_tap + col_count,
                        :,
                    ]
                )
    columns = jnp.concatenate(windows, axis=-1).reshape(-1, 27 * channels)
    convolved = jnp.dot(
        columns, conv_weight.reshape(27 * channels, channels), preferred_element_type=jnp.float32
    )
    decoded = features + conv_bias + convolved.reshape(frame_count, rows_here, col_count, channels)
    return (attended, decoded.astype(jnp.bfloat16))


def solution(mesh):
    placed = (
        P(("group", "span"), None),
        P(None, ("group", "span"), None),
        P("group"),
        P("group", None),
        P("group"),
        P("group", "span", None, None),
        P("group", "span", None, None),
        P(),
        P(),
        P(),
    )
    return jax.shard_map(
        shards,
        mesh=mesh,
        in_specs=placed,
        out_specs=(P(("group", "span"), None), P("group", "span", None, None)),
        check_vma=False,
    )
```

profile of v0, /device:TPU:0, one launch (start us, length us, event | category | flops | bytes accessed | tf_op | source)
XLA Modules:
  0.0 297.3 jit_solution(355756754644313053)
XLA Ops:
  12.2 3.7 %collective-permute-start.9 = (bf16[5,1,52,384]{3,2,0,1:T(8,128)(2,1)}, bf16[5,1,52,384]{3,2,0,1:T(8,128)(2,1)}, u32[]{:S(2)}, u32[]{:S(2)}) collective-permute-start(bf16[5,1,52,384]{3,2,0,1:T(8,128)(2,1)} %pad_maximum_fusion.2), channel_id=1, source_target_pairs={{0,1},{1,2},{2,3},{3,4},{4,5},{5,6},{6,7},{7,8},{8,9},{9,10},{10,1... | collective-permute-start | bytes 599048 | tf_op jit(solution)/shard_map/ppermute | solution.py:22
  15.9 3.0 copy.23
  23.3 8.1 %collective-permute-start.1 = (bf16[2,256,2560]{1,2,0:T(8,128)(2,1)S(1)}, bf16[2,256,2560]{1,2,0:T(8,128)(2,1)}, u32[]{:S(2)}, u32[]{:S(2)}) collective-permute-start(bf16[2,256,2560]{1,2,0:T(8,128)(2,1)S(1)} %copy.23), channel_id=1, source_target_pairs={{0,2},{4,6},{8,10},{12,14},{1,3},{5,7},{9,11},{13,15},{16,18},{20,... | collective-permute-start | bytes 7864328 | tf_op jit(solution)/shard_map/ppermute | solution.py:31
  33.4 2.2 fusion.55
  43.6 2.5 slice_bitcast_fusion.2
  46.8 3.6 %collective-permute-start = (bf16[2,256,2560]{1,2,0:T(8,128)(2,1)S(1)}, bf16[2,256,2560]{1,2,0:T(8,128)(2,1)}, u32[]{:S(2)}, u32[]{:S(2)}) collective-permute-start(bf16[2,256,2560]{1,2,0:T(8,128)(2,1)S(1)} %copy.23), channel_id=1, source_target_pairs={{0,1},{4,5},{8,9},{12,13},{2,3},{6,7},{10,11},{14,15},{16,17},{20,... | collective-permute-start | bytes 7864328 | tf_op jit(solution)/shard_map/ppermute | solution.py:31
  58.8 35.7 %collective-permute-done.4 = bf16[2,256,2560]{1,2,0:T(8,128)(2,1)S(1)} collective-permute-done((bf16[2,256,2560]{1,2,0:T(8,128)(2,1)}, bf16[2,256,2560]{1,2,0:T(8,128)(2,1)S(1)}, u32[]{:S(2)}, u32[]{:S(2)}) %collective-permute-start.4) | collective-permute-done | bytes 2621472 | tf_op jit(solution)/shard_map/ppermute | solution.py:31
  94.5 21.8 %collective-permute-done.6 = bf16[2,256,2560]{1,2,0:T(8,128)(2,1)S(1)} collective-permute-done((bf16[2,256,2560]{1,2,0:T(8,128)(2,1)}, bf16[2,256,2560]{1,2,0:T(8,128)(2,1)S(1)}, u32[]{:S(2)}, u32[]{:S(2)}) %collective-permute-start.6) | collective-permute-done | bytes 2621472 | tf_op jit(solution)/shard_map/ppermute | solution.py:31
  116.3 3.1 %pad_maximum_fusion.1 = bf16[2,2,256,2560]{2,3,1,0:T(8,128)(2,1)} fusion(bf16[1,2,256,2560]{2,3,1,0:T(8,128)(2,1)S(1)} %bitcast.138, bf16[1,2,256,2560]{2,3,1,0:T(8,128)(2,1)S(1)} %bitcast.137), kind=kLoop, calls=%fused_computation.13 | loop fusion | flops 2621440 | bytes 10485760 | tf_op jit(solution)/shard_map/stack | solution.py:50
  120.3 3.7 %collective-permute-start.7 = (bf16[2,2,256,2560]{2,3,1,0:T(8,128)(2,1)}, bf16[2,2,256,2560]{2,3,1,0:T(8,128)(2,1)}, u32[]{:S(2)}, u32[]{:S(2)}) collective-permute-start(bf16[2,2,256,2560]{2,3,1,0:T(8,128)(2,1)} %pad_maximum_fusion.1), channel_id=1, source_target_pairs={{0,1},{4,5},{8,9},{12,13},{16,17},{20,21},{24,25},{28,29}} | collective-permute-start | bytes 15728648 | tf_op jit(solution)/shard_map/ppermute | solution.py:31
  127.4 2.2 collective-permute-start.2
  129.6 2.7 fusion.30
  132.3 48.4 %all-reduce.4.cloned.1.call-done = bf16[256,2560]{0,1:T(8,128)(2,1)} async-done(((bf16[256,2560]{0,1:T(8,128)(2,1)}), bf16[256,2560]{0,1:T(8,128)(2,1)}) %all-reduce.4.cloned.1.call-update) | async-done | bytes 1310736 | tf_op jit(solution)/shard_map/psum | solution.py:14
  187.4 6.4 %select_select_fusion = (bf16[2,256,2560]{1,2,0:T(8,128)(2,1)S(1)}, bf16[2,256,2560]{1,2,0:T(8,128)(2,1)S(1)}, bf16[2,256,2560]{1,2,0:T(8,128)(2,1)S(1)}) fusion(bf16[2,256,2560]{1,2,0:T(8,128)(2,1)} %collective-permute-done.1, bf16[2,256,2560]{1,2,0:T(8,128)(2,1)S(1)} %copy-done.4, bf16[2,2,256,2560]{2,3,1,0:T(8,128)(2,1)} %collective-permute-done.7, ...), kind=kLoop, calls=%fused_computation.16 | loop fusion | flops 11796480 | bytes 31457284 | tf_op jit(solution)/shard_map/jit(_where)/select_n | solution.py:55
  195.3 3.0 fusion.52
  198.3 2.7 fusion.57
  200.9 6.2 %bitcast_reduce_fusion = (f32[10,256]{1,0:T(8,128)S(1)}, f32[10,256]{1,0:T(8,128)S(1)}, f32[10,1024,256]{2,1,0:T(8,128)}) fusion(pred[1024]{0:T(1024)(128)(4,1)S(1)} %pad_add_fusion, f32[10,1024,256]{2,1,0:T(8,128)S(1)} %fusion.57, bf16[1024,10,128]{0,2,1:T(8,128)(2,1)S(1)} %bitcast.139, bf16[256,10,128]{0,2,1:T(8,128)(2,1)S(1)} %bitcast.142), kind=kOutput, calls=%fused_computation.2 | convolution fusion | flops 686812160 | bytes 24269824 | tf_op jit(solution)/shard_map/qhd,khd->hqk/dot_general | solution.py:65
  208.3 7.4 %fusion.3 = (f32[10,256]{1,0:T(8,128)S(1)}, f32[10,256]{1,0:T(8,128)S(1)}) fusion(f32[10,1024,256]{2,1,0:T(8,128)} %get-tuple-element.51, f32[10,256]{1,0:T(8,128)S(1)} %max.17, pred[1024]{0:T(1024)(128)(4,1)S(1)} %pad_add_fusion, f32[10,256]{1,0:T(8,128)S(1)} %max.16, f32[10,1024,256]{2,1,0:T(8,128)S(1)} %fusion.57), kind=kLoop, calls=%fused_computation.12 | loop fusion | flops 20966400 | bytes 21013504 | tf_op jit(solution)/shard_map/reduce_sum | solution.py:114
  215.7 9.1 %fusion.5 = f32[10,256,128]{2,1,0:T(8,128)} fusion(bf16[1024,10,128]{0,2,1:T(8,128)(2,1)} %bitcast.146, f32[10,1024,256]{2,1,0:T(8,128)} %get-tuple-element.51, f32[10,256]{1,0:T(8,128)S(1)} %add.107, f32[10,256]{1,0:T(8,128)S(1)} %max.17, pred[1024]{0:T(1024)(128)(4,1)S(1)} %pad_add_fusion), kind=kOutput, calls=%fused_computation.15 | convolution fusion | flops 684195840 | bytes 14439424 | tf_op jit(solution)/shard_map/hqk,khd->hqd/dot_general | solution.py:117
  224.8 6.1 %fusion.4 = f32[10,256,128]{2,1,0:T(8,128)} fusion(bf16[1024,10,128]{0,2,1:T(8,128)(2,1)} %bitcast.145, f32[10,1024,256]{2,1,0:T(8,128)S(1)} %fusion.57, f32[10,256]{1,0:T(8,128)S(1)} %add.106, f32[10,256]{1,0:T(8,128)S(1)} %max.16, pred[1024]{0:T(1024)(128)(4,1)S(1)} %pad_add_fusion), kind=kOutput, calls=%fused_computation.14 | convolution fusion | flops 684195840 | bytes 14439424 | tf_op jit(solution)/shard_map/hqk,khd->hqd/dot_general | solution.py:117
  230.9 3.0 %divide_convert_fusion.4 = (bf16[10,256,256]{1,2,0:T(8,128)(2,1)S(1)}, bf16[10,256,256]{1,2,0:T(8,128)(2,1)S(1)}) fusion(f32[10,256,256]{2,1,0:T(8,128)} %copy-done, f32[10,256]{1,0:T(8,128)S(1)} %add.107, f32[10,256]{1,0:T(8,128)S(1)} %max.17, pred[256]{0:T(512)(128)(4,1)S(1)} %compare_and_fusion, f32[10,256]{1,0:T(8,128)S(1)} %add.106, ...), kind=kLoop, calls=%fused_computation.33 | loop fusion | flops 6553600 | bytes 7905536 | tf_op jit(solution)/shard_map/convert_element_type | solution.py:116
  233.8 43.7 %all-reduce.6.cloned.1.call-done = bf16[256,2560]{1,0:T(8,128)(2,1)} async-done(((bf16[256,2560]{1,0:T(8,128)(2,1)}), bf16[256,2560]{1,0:T(8,128)(2,1)}) %all-reduce.6.cloned.1.call-update) | async-done | bytes 1310736 | tf_op jit(solution)/shard_map/psum | solution.py:14
  277.6 2.2 fusion.53
  282.0 2.9 fusion.18
  (105 shorter events, 46.8 us)
Async XLA Ops:
  7.2 173.5 %all-reduce.4.cloned.1.call-start = ((), (), s32[]{:S(2)}) async-start(), calls=%async_computation | async-start | bytes 2621440 | tf_op jit(solution)/shard_map/psum | solution.py:14
  10.9 35.8 %collective-permute-start.10 = (bf16[5,1,52,384]{3,2,0,1:T(8,128)(2,1)}, bf16[5,1,52,384]{3,2,0,1:T(8,128)(2,1)}, u32[]{:S(2)}, u32[]{:S(2)}) collective-permute-start(bf16[5,1,52,384]{3,2,0,1:T(8,128)(2,1)} %pad_maximum_fusion.2), channel_id=1, source_target_pairs={{1,0},{2,1},{3,2},{4,3},{5,4},{6,5},{7,6},{8,7},{9,8},{10,9},{11,1... | collective-permute-start | bytes 599048 | tf_op jit(solution)/shard_map/ppermute | solution.py:25
  12.2 38.1 %collective-permute-start.9 = (bf16[5,1,52,384]{3,2,0,1:T(8,128)(2,1)}, bf16[5,1,52,384]{3,2,0,1:T(8,128)(2,1)}, u32[]{:S(2)}, u32[]{:S(2)}) collective-permute-start(bf16[5,1,52,384]{3,2,0,1:T(8,128)(2,1)} %pad_maximum_fusion.2), channel_id=1, source_target_pairs={{0,1},{1,2},{2,3},{3,4},{4,5},{5,6},{6,7},{7,8},{8,9},{9,10},{10,1... | collective-permute-start | bytes 599048 | tf_op jit(solution)/shard_map/ppermute | solution.py:22
  18.9 34.9 %collective-permute-start.3 = (bf16[2,256,2560]{1,2,0:T(8,128)(2,1)S(1)}, bf16[2,256,2560]{1,2,0:T(8,128)(2,1)}, u32[]{:S(2)}, u32[]{:S(2)}) collective-permute-start(bf16[2,256,2560]{1,2,0:T(8,128)(2,1)S(1)} %copy.23), channel_id=1, source_target_pairs={{3,6},{7,10},{11,14},{15,2},{19,22},{23,26},{27,30},{31,18}} | collective-permute-start | bytes 7864328 | tf_op jit(solution)/shard_map/ppermute | solution.py:31
  21.1 34.0 %collective-permute-start.5 = (bf16[2,256,2560]{1,2,0:T(8,128)(2,1)S(1)}, bf16[2,256,2560]{1,2,0:T(8,128)(2,1)}, u32[]{:S(2)}, u32[]{:S(2)}) collective-permute-start(bf16[2,256,2560]{1,2,0:T(8,128)(2,1)S(1)} %copy.23), channel_id=1, source_target_pairs={{2,1},{6,5},{10,9},{14,13},{18,17},{22,21},{26,25},{30,29}} | collective-permute-start | bytes 7864328 | tf_op jit(solution)/shard_map/ppermute | solution.py:31
  23.3 104.0 %collective-permute-start.1 = (bf16[2,256,2560]{1,2,0:T(8,128)(2,1)S(1)}, bf16[2,256,2560]{1,2,0:T(8,128)(2,1)}, u32[]{:S(2)}, u32[]{:S(2)}) collective-permute-start(bf16[2,256,2560]{1,2,0:T(8,128)(2,1)S(1)} %copy.23), channel_id=1, source_target_pairs={{0,2},{4,6},{8,10},{12,14},{1,3},{5,7},{9,11},{13,15},{16,18},{20,... | collective-permute-start | bytes 7864328 | tf_op jit(solution)/shard_map/ppermute | solution.py:31
  33.2 3.5 %copy-start.10 = (s32[16,3]{0,1:T(4,128)S(1)}, s32[16,3]{0,1:T(4,128)}, u32[]{:S(2)}) copy-start(s32[16,3]{0,1:T(4,128)} %param.13) | copy-start | bytes 580
  33.3 244.3 %all-reduce.6.cloned.1.call-start = ((), (), s32[]{:S(2)}) async-start(), calls=%async_computation.1 | async-start | bytes 2621440 | tf_op jit(solution)/shard_map/psum | solution.py:14
  33.4 7.1 %copy-start.7 = (s32[16]{0:T(128)S(1)}, s32[16]{0:T(128)}, u32[]{:S(2)}) copy-start(s32[16]{0:T(128)} %param.14) | copy-start | bytes 196
  46.8 138.2 %collective-permute-start = (bf16[2,256,2560]{1,2,0:T(8,128)(2,1)S(1)}, bf16[2,256,2560]{1,2,0:T(8,128)(2,1)}, u32[]{:S(2)}, u32[]{:S(2)}) collective-permute-start(bf16[2,256,2560]{1,2,0:T(8,128)(2,1)S(1)} %copy.23), channel_id=1, source_target_pairs={{0,1},{4,5},{8,9},{12,13},{2,3},{6,7},{10,11},{14,15},{16,17},{20,... | collective-permute-start | bytes 7864328 | tf_op jit(solution)/shard_map/ppermute | solution.py:31
  50.3 134.6 %collective-permute-start.8 = (bf16[2,256,2560]{1,2,0:T(8,128)(2,1)S(1)}, bf16[2,256,2560]{1,2,0:T(8,128)(2,1)}, u32[]{:S(2)}, u32[]{:S(2)}) collective-permute-start(bf16[2,256,2560]{1,2,0:T(8,128)(2,1)S(1)} %copy.23), channel_id=1, source_target_pairs={{1,4},{5,8},{9,12},{13,0},{17,20},{21,24},{25,28},{29,16}} | collective-permute-start | bytes 7864328 | tf_op jit(solution)/shard_map/ppermute | solution.py:31
  53.9 40.6 %collective-permute-start.4 = (bf16[2,256,2560]{1,2,0:T(8,128)(2,1)}, bf16[2,256,2560]{1,2,0:T(8,128)(2,1)S(1)}, u32[]{:S(2)}, u32[]{:S(2)}) collective-permute-start(bf16[2,256,2560]{1,2,0:T(8,128)(2,1)} %collective-permute-done.3), channel_id=1, source_target_pairs={{2,0},{6,4},{10,8},{14,12},{18,16},{22,20},{26,24},{30,28}} | collective-permute-start | bytes 7864328 | tf_op jit(solution)/shard_map/ppermute | solution.py:31
  55.2 61.2 %collective-permute-start.6 = (bf16[2,256,2560]{1,2,0:T(8,128)(2,1)}, bf16[2,256,2560]{1,2,0:T(8,128)(2,1)S(1)}, u32[]{:S(2)}, u32[]{:S(2)}) collective-permute-start(bf16[2,256,2560]{1,2,0:T(8,128)(2,1)} %collective-permute-done.5), channel_id=1, source_target_pairs={{1,4},{5,8},{9,12},{13,0},{17,20},{21,24},{25,28},{29,16}} | collective-permute-start | bytes 7864328 | tf_op jit(solution)/shard_map/ppermute | solution.py:31
  58.6 71.0 %slice-start = ((s8[7962624]{0:T(1024)(128)(4,1)}), s8[4194304]{0:T(1024)(128)(4,1)S(1)}, s32[]{:S(2)}) async-start(s8[7962624]{0:T(1024)(128)(4,1)} %bitcast.134), calls=%async_computation.2 | async-start | bytes 8388608
  94.5 25.0 %copy-start.1 = (bf16[2,256,2560]{1,2,0:T(8,128)(2,1)}, bf16[2,256,2560]{1,2,0:T(8,128)(2,1)S(1)}, u32[]{:S(2)}) copy-start(bf16[2,256,2560]{1,2,0:T(8,128)(2,1)S(1)} %collective-permute-done.4) | copy-start | bytes 7864324
  116.3 4.0 %copy-start.3 = (bf16[2,256,2560]{1,2,0:T(8,128)(2,1)}, bf16[2,256,2560]{1,2,0:T(8,128)(2,1)S(1)}, u32[]{:S(2)}) copy-start(bf16[2,256,2560]{1,2,0:T(8,128)(2,1)S(1)} %collective-permute-done.6) | copy-start | bytes 7864324
  116.3 9.8 %copy-start.6 = (bf16[3,1,52,384]{3,2,1,0:T(8,128)(2,1)S(1)}, bf16[3,1,52,384]{3,2,1,0:T(8,128)(2,1)}, u32[]{:S(2)}) copy-start(bf16[3,1,52,384]{3,2,1,0:T(8,128)(2,1)} %param.15) | copy-start | bytes 359428
  116.3 9.8 %copy-start.8 = (f32[384]{0:T(512)S(1)}, f32[384]{0:T(512)}, u32[]{:S(2)}) copy-start(f32[384]{0:T(512)} %param.17) | copy-start | bytes 4612
  116.3 13.3 %slice-start.1 = ((s8[7962624]{0:T(1024)(128)(4,1)}), s8[3768320]{0:T(1024)(128)(4,1)S(1)}, s32[]{:S(2)}) async-start(s8[7962624]{0:T(1024)(128)(4,1)} %bitcast.134), calls=%async_computation.3 | async-start | bytes 7536640
  120.3 9.3 %copy-start.9 = (f32[384]{0:T(512)S(1)}, f32[384]{0:T(512)}, u32[]{:S(2)}) copy-start(f32[384]{0:T(512)} %param.19) | copy-start | bytes 4612
  120.3 64.7 %collective-permute-start.7 = (bf16[2,2,256,2560]{2,3,1,0:T(8,128)(2,1)}, bf16[2,2,256,2560]{2,3,1,0:T(8,128)(2,1)}, u32[]{:S(2)}, u32[]{:S(2)}) collective-permute-start(bf16[2,2,256,2560]{2,3,1,0:T(8,128)(2,1)} %pad_maximum_fusion.1), channel_id=1, source_target_pairs={{0,1},{4,5},{8,9},{12,13},{16,17},{20,21},{24,25},{28,29}} | collective-permute-start | bytes 15728648 | tf_op jit(solution)/shard_map/ppermute | solution.py:31
  127.4 57.6 %collective-permute-start.2 = (bf16[2,256,2560]{1,2,0:T(8,128)(2,1)}, bf16[2,256,2560]{1,2,0:T(8,128)(2,1)}, u32[]{:S(2)}, u32[]{:S(2)}) collective-permute-start(bf16[2,256,2560]{1,2,0:T(8,128)(2,1)} %collective-permute-done.1), channel_id=1, source_target_pairs={{3,2},{7,6},{11,10},{15,14},{2,3},{6,7},{10,11},{14,15},{19,18},{2... | collective-permute-start | bytes 7864328 | tf_op jit(solution)/shard_map/ppermute | solution.py:31
  183.9 3.5 %copy-start.4 = (bf16[2,256,2560]{1,2,0:T(8,128)(2,1)S(1)}, bf16[2,256,2560]{1,2,0:T(8,128)(2,1)}, u32[]{:S(2)}) copy-start(bf16[2,256,2560]{1,2,0:T(8,128)(2,1)} %copy-done.3) | copy-start | bytes 7864324
  184.9 22.2 %copy-start = (f32[10,256,256]{2,1,0:T(8,128)}, f32[10,256,256]{2,1,0:T(8,128)S(1)}, u32[]{:S(2)}) copy-start(f32[10,256,256]{2,1,0:T(8,128)S(1)} %get-tuple-element.52) | copy-start | bytes 7864324
  (2 other events, 3.2 us)
Sparse Core Ops, SparseCore 0:
  33.4 147.2 all-reduce.3
  184.2 93.3 all-reduce.5
where the time goes:
time: 298 us; the launch traced here: 297 us
  waiting for transfers between devices  150 us (50%)
  local copies, waits for them, and re-layouts  34 us (11%)
  matrix products  33 us (11%)
  other arithmetic  32.4 us (11%)
  starting transfers between devices  31 us (10%)
  between operations  17.1 us (6%)
    psum x2, waiting for transfers between devices, spread(): return lax.psum(block, axis)  92.1 us
    ppermute x9, waiting for transfers between devices, move(): return lax.ppermute(value, 'span', pairs)  57.6 us
    ppermute x9, starting transfers between devices, move(): return lax.ppermute(value, 'span', pairs)  25.9 us
    unnamed x54, local copies, waits for them, and re-layouts  17.4 us
    dot_general x2, matrix products, shards(): jnp.einsum('hqk,khd->hqd', w_probs, wv, preferred_element_type=jnp.float32)  15.1 us
    dot_general x4, matrix products, part_stats(): jnp.einsum('qhd,khd->hqk', q, k, preferred_element_type=jnp.float32) * scale  10.4 us
    reduce_sum x1, other arithmetic, shards(): jnp.sum(w_exp, axis=-1, keepdims=True)  7.39 us
    select_n x1, other arithmetic, pick(): out = jnp.where(lane == l, options[l], out)  6.38 us
  transfers between devices with their start and end apart: 13, of which 4 were waited for; matrix products, arithmetic and copies ran while one was open for 27% of the time, Pallas kernels for 0%

commit v1 on v0

--- a/solution.py
+++ b/solution.py
@@ -11,7 +11,7 @@
 
 def spread(block, axis, source):
     block = jnp.where(lax.axis_index(axis) == source, block, jnp.zeros_like(block))
-    return lax.psum(block, axis)
+    return jnp.sum(lax.all_gather(block, axis), axis=0)
 
 
 def extended_2(block, sides, width):

time: 298 us -> 422 us (1.42)
  starting transfers between devices: 31 us -> 158 us
  other arithmetic: 32.4 us -> 58.7 us
  waiting for transfers between devices: 150 us -> 125 us
    all_gather x0 -> x2, waiting for transfers between devices: none -> 112 us  [spread(): return jnp.sum(lax.all_gather(block, axis), axis=0)]
    psum x2 -> x0, waiting for transfers between devices: 92.1 us -> none  [spread(): return lax.psum(block, axis)]
    ppermute x1, starting transfers between devices: 3.73 us -> 81.3 us  [extended_2(): lax.ppermute(lax.slice_in_dim(block, block.shape[dim] - width, None, axis...]
    ppermute x9, starting transfers between devices: 25.9 us -> 75.5 us  [move(): return lax.ppermute(value, 'span', pairs)]
    ppermute x9, waiting for transfers between devices: 57.6 us -> 13.3 us  [move(): return lax.ppermute(value, 'span', pairs)]
    reduce_sum x0 -> x2, other arithmetic: none -> 23.5 us  [spread(): return jnp.sum(lax.all_gather(block, axis), axis=0)]
    unnamed x54 -> x60, local copies, waits for them, and re-layouts: 17.4 us -> 17.2 us
  transfers between devices with their start and end apart: 13 -> 13, of which waited for: 4 -> 2; matrix products, arithmetic and copies ran while one was open for 27% -> 19% of each run, Pallas kernels for 0% -> 0%
where the time goes in v1:
time: 422 us; the launch traced here: 421 us
  starting transfers between devices  158 us (37%)
  waiting for transfers between devices  125 us (30%)
  other arithmetic  58.7 us (14%)
  matrix products  32 us (8%)
  local copies, waits for them, and re-layouts  30 us (7%)
  between operations  17.1 us (4%)
    all_gather x2, waiting for transfers between devices, spread(): return jnp.sum(lax.all_gather(block, axis), axis=0)  112 us
    ppermute x1, starting transfers between devices, extended_2(): lax.ppermute(lax.slice_in_dim(block, block.shape[dim] - width, None, axis...  81.3 us
    ppermute x9, starting transfers between devices, move(): return lax.ppermute(value, 'span', pairs)  75.5 us
    reduce_sum x2, other arithmetic, spread(): return jnp.sum(lax.all_gather(block, axis), axis=0)  23.5 us
    unnamed x60, local copies, waits for them, and re-layouts  17.2 us
    dot_general x2, matrix products, shards(): jnp.einsum('hqk,khd->hqd', w_probs, wv, preferred_element_type=jnp.float32)  15.1 us
    ppermute x9, waiting for transfers between devices, move(): return lax.ppermute(value, 'span', pairs)  13.3 us
    dot_general x4, matrix products, part_stats(): jnp.einsum('qhd,khd->hqk', q, k, preferred_element_type=jnp.float32) * scale  10.1 us
  transfers between devices with their start and end apart: 13, of which 2 were waited for; matrix products, arithmetic and copies ran while one was open for 19% of the time, Pallas kernels for 0%

profile of v1, /device:TPU:0, one launch (start us, length us, event | category | flops | bytes accessed | tf_op | source)
XLA Modules:
  0.0 421.2 jit_solution(5782975408140804499)
XLA Ops:
  7.9 3.4 slice_select_fusion
  11.4 111.6 %all-gather.4.cloned.1.call-done = bf16[16,256,2560]{2,1,0:T(8,128)(2,1)} async-done(((bf16[1,256,2560]{2,1,0:T(8,128)(2,1)}), bf16[16,256,2560]{2,1,0:T(8,128)(2,1)}) %all-gather.4.cloned.1.call-update) | async-done | bytes 20971536 | tf_op jit(solution)/shard_map/all_gather | solution.py:14
  123.0 12.3 %reduce_sum.69 = bf16[256,2560]{1,0:T(8,128)(2,1)} reduce(bf16[16,256,2560]{2,1,0:T(8,128)(2,1)} %all-gather.4.cloned.1.call-done, bf16[]{:T(256)} %constant.60.clone.1), dimensions={0}, to_apply=%region_0.1 | reduce | flops 9830400 | bytes 22282242 | tf_op jit(solution)/shard_map/reduce_sum | solution.py:14
  137.5 2.6 copy.56
  140.1 2.3 collective-permute-start.5
  142.4 2.1 collective-permute-start.3
  144.5 5.7 %collective-permute-start.1 = (bf16[2,256,2560]{1,2,0:T(8,128)(2,1)}, bf16[2,256,2560]{1,2,0:T(8,128)(2,1)}, u32[]{:S(2)}, u32[]{:S(2)}) collective-permute-start(bf16[2,256,2560]{1,2,0:T(8,128)(2,1)} %copy.56), channel_id=1, source_target_pairs={{0,2},{4,6},{8,10},{12,14},{1,3},{5,7},{9,11},{13,15},{16,18},{20,... | collective-permute-start | bytes 7864328 | tf_op jit(solution)/shard_map/ppermute | solution.py:31
  155.2 81.3 %collective-permute-start.9 = (bf16[5,1,52,384]{3,2,0,1:T(8,128)(2,1)}, bf16[5,1,52,384]{3,2,0,1:T(8,128)(2,1)}, u32[]{:S(2)}, u32[]{:S(2)}) collective-permute-start(bf16[5,1,52,384]{3,2,0,1:T(8,128)(2,1)} %pad_maximum_fusion.2), channel_id=1, source_target_pairs={{0,1},{1,2},{2,3},{3,4},{4,5},{5,6},{6,7},{7,8},{8,9},{9,10},{10,1... | collective-permute-start | bytes 599048 | tf_op jit(solution)/shard_map/ppermute | solution.py:22
  236.5 2.2 fusion.54
  249.0 58.9 %collective-permute-start = (bf16[2,256,2560]{1,2,0:T(8,128)(2,1)}, bf16[2,256,2560]{1,2,0:T(8,128)(2,1)}, u32[]{:S(2)}, u32[]{:S(2)}) collective-permute-start(bf16[2,256,2560]{1,2,0:T(8,128)(2,1)} %copy.56), channel_id=1, source_target_pairs={{0,1},{4,5},{8,9},{12,13},{2,3},{6,7},{10,11},{14,15},{16,17},{20,... | collective-permute-start | bytes 7864328 | tf_op jit(solution)/shard_map/ppermute | solution.py:31
  310.4 5.0 %pad_maximum_fusion.1 = bf16[2,2,256,2560]{2,3,1,0:T(8,128)(2,1)} fusion(bf16[1,2,256,2560]{2,3,1,0:T(8,128)(2,1)S(1)} %bitcast.137, bf16[1,2,256,2560]{2,3,1,0:T(8,128)(2,1)} %bitcast.10), kind=kLoop, calls=%fused_computation.13 | loop fusion | flops 2621440 | bytes 10485760 | tf_op jit(solution)/shard_map/stack | solution.py:50
  323.5 2.7 fusion.29
  326.1 13.3 %collective-permute-done.8 = bf16[2,256,2560]{1,2,0:T(8,128)(2,1)S(1)} collective-permute-done((bf16[2,256,2560]{1,2,0:T(8,128)(2,1)}, bf16[2,256,2560]{1,2,0:T(8,128)(2,1)S(1)}, u32[]{:S(2)}, u32[]{:S(2)}) %collective-permute-start.8) | collective-permute-done | bytes 2621472 | tf_op jit(solution)/shard_map/ppermute | solution.py:31
  340.9 4.8 %select_select_fusion = (bf16[2,256,2560]{1,2,0:T(8,128)(2,1)S(1)}, bf16[2,256,2560]{1,2,0:T(8,128)(2,1)S(1)}, bf16[2,256,2560]{1,2,0:T(8,128)(2,1)S(1)}) fusion(bf16[2,256,2560]{1,2,0:T(8,128)(2,1)} %collective-permute-done.1, bf16[2,256,2560]{1,2,0:T(8,128)(2,1)S(1)} %collective-permute-done.6, bf16[2,2,256,2560]{2,3,1,0:T(8,128)(2,1)S(1)} %collective-permute-done.7, ...), kind=kLoop, calls=%fused_computation.16 | loop fusion | flops 11796480 | bytes 31457284 | tf_op jit(solution)/shard_map/jit(_where)/select_n | solution.py:55
  345.8 4.0 pad_maximum_fusion
  349.8 2.9 fusion.51
  354.3 7.0 %bitcast_reduce_fusion = (f32[10,256]{1,0:T(8,128)S(1)}, f32[10,256]{1,0:T(8,128)S(1)}, f32[10,1024,256]{2,1,0:T(8,128)}) fusion(pred[1024]{0:T(1024)(128)(4,1)S(1)} %pad_add_fusion, f32[10,1024,256]{2,1,0:T(8,128)S(1)} %fusion.56, bf16[1024,10,128]{0,2,1:T(8,128)(2,1)S(1)} %bitcast.138, bf16[256,10,128]{0,2,1:T(8,128)(2,1)S(1)} %bitcast.140), kind=kOutput, calls=%fused_computation.2 | convolution fusion | flops 686812160 | bytes 24269824 | tf_op jit(solution)/shard_map/qhd,khd->hqk/dot_general | solution.py:65
  368.4 7.3 %fusion.3 = (f32[10,256]{1,0:T(8,128)S(1)}, f32[10,256]{1,0:T(8,128)S(1)}) fusion(f32[10,1024,256]{2,1,0:T(8,128)} %get-tuple-element.55, f32[10,256]{1,0:T(8,128)S(1)} %max.17, pred[1024]{0:T(1024)(128)(4,1)S(1)} %pad_add_fusion, f32[10,256]{1,0:T(8,128)S(1)} %max.16, f32[10,1024,256]{2,1,0:T(8,128)S(1)} %copy-done.1), kind=kLoop, calls=%fused_computation.12 | loop fusion | flops 20966400 | bytes 21013504 | tf_op jit(solution)/shard_map/reduce_sum | solution.py:114
  375.8 2.3 divide_convert_fusion.4
  378.1 6.1 %fusion.4 = f32[10,256,128]{2,1,0:T(8,128)} fusion(bf16[1024,10,128]{0,2,1:T(8,128)(2,1)} %bitcast.145, f32[10,1024,256]{2,1,0:T(8,128)S(1)} %copy-done.1, f32[10,256]{1,0:T(8,128)S(1)} %add.102, f32[10,256]{1,0:T(8,128)S(1)} %max.16, pred[1024]{0:T(1024)(128)(4,1)S(1)} %pad_add_fusion), kind=kOutput, calls=%fused_computation.14 | convolution fusion | flops 684195840 | bytes 14439424 | tf_op jit(solution)/shard_map/hqk,khd->hqd/dot_general | solution.py:117
  384.2 9.0 %fusion.5 = f32[10,256,128]{2,1,0:T(8,128)} fusion(bf16[1024,10,128]{0,2,1:T(8,128)(2,1)} %bitcast.144, f32[10,1024,256]{2,1,0:T(8,128)} %get-tuple-element.55, f32[10,256]{1,0:T(8,128)S(1)} %add.103, f32[10,256]{1,0:T(8,128)S(1)} %max.17, pred[1024]{0:T(1024)(128)(4,1)S(1)} %pad_add_fusion), kind=kOutput, calls=%fused_computation.15 | convolution fusion | flops 684195840 | bytes 14439424 | tf_op jit(solution)/shard_map/hqk,khd->hqd/dot_general | solution.py:117
  393.2 11.2 %reduce_sum.70 = bf16[256,2560]{1,0:T(8,128)(2,1)S(1)} reduce(bf16[16,256,2560]{2,1,0:T(8,128)(2,1)} %bitcast.133, bf16[]{:T(256)} %constant.60.clone.1), dimensions={0}, to_apply=%region_1.2 | reduce | flops 9830400 | bytes 22282242 | tf_op jit(solution)/shard_map/reduce_sum | solution.py:14
  406.6 2.3 fusion.17
  410.3 1.9 fusion.18
  (114 shorter events, 41.6 us)
Async XLA Ops:
  7.2 115.8 %all-gather.4.cloned.1.call-start = ((), (), s32[]{:S(2)}) async-start(), calls=%async_computation | async-start | bytes 22282240 | tf_op jit(solution)/shard_map/all_gather | solution.py:14
  11.3 381.9 %all-gather.6.cloned.1.call-start = ((), (), s32[]{:S(2)}) async-start(), calls=%async_computation.1 | async-start | bytes 22282240 | tf_op jit(solution)/shard_map/all_gather | solution.py:14
  137.5 12.8 %copy-start.7 = (bf16[3,1,52,384]{3,2,1,0:T(8,128)(2,1)S(1)}, bf16[3,1,52,384]{3,2,1,0:T(8,128)(2,1)}, u32[]{:S(2)}) copy-start(bf16[3,1,52,384]{3,2,1,0:T(8,128)(2,1)} %param.15) | copy-start | bytes 359428
  137.5 15.5 %copy-start.11 = (f32[384]{0:T(512)S(1)}, f32[384]{0:T(512)}, u32[]{:S(2)}) copy-start(f32[384]{0:T(512)} %param.17) | copy-start | bytes 4612
  137.5 15.7 %copy-start.9 = (bf16[2,1,52,384]{3,0,2,1:T(2,128)(2,1)S(1)}, bf16[2,1,52,384]{3,0,2,1:T(2,128)(2,1)}, u32[]{:S(2)}) copy-start(bf16[2,1,52,384]{3,0,2,1:T(2,128)(2,1)} %param.16) | copy-start | bytes 239620
  140.1 99.8 %copy-start.13 = (s32[16,3]{0,1:T(4,128)S(1)}, s32[16,3]{0,1:T(4,128)}, u32[]{:S(2)}) copy-start(s32[16,3]{0,1:T(4,128)} %param.13) | copy-start | bytes 580
  140.1 10.3 %collective-permute-start.5 = (bf16[2,256,2560]{1,2,0:T(8,128)(2,1)}, bf16[2,256,2560]{1,2,0:T(8,128)(2,1)}, u32[]{:S(2)}, u32[]{:S(2)}) collective-permute-start(bf16[2,256,2560]{1,2,0:T(8,128)(2,1)} %copy.56), channel_id=1, source_target_pairs={{2,1},{6,5},{10,9},{14,13},{18,17},{22,21},{26,25},{30,29}} | collective-permute-start | bytes 7864328 | tf_op jit(solution)/shard_map/ppermute | solution.py:31
  142.4 9.3 %collective-permute-start.3 = (bf16[2,256,2560]{1,2,0:T(8,128)(2,1)}, bf16[2,256,2560]{1,2,0:T(8,128)(2,1)}, u32[]{:S(2)}, u32[]{:S(2)}) collective-permute-start(bf16[2,256,2560]{1,2,0:T(8,128)(2,1)} %copy.56), channel_id=1, source_target_pairs={{3,6},{7,10},{11,14},{15,2},{19,22},{23,26},{27,30},{31,18}} | collective-permute-start | bytes 7864328 | tf_op jit(solution)/shard_map/ppermute | solution.py:31
  144.5 175.8 %collective-permute-start.1 = (bf16[2,256,2560]{1,2,0:T(8,128)(2,1)}, bf16[2,256,2560]{1,2,0:T(8,128)(2,1)}, u32[]{:S(2)}, u32[]{:S(2)}) collective-permute-start(bf16[2,256,2560]{1,2,0:T(8,128)(2,1)} %copy.56), channel_id=1, source_target_pairs={{0,2},{4,6},{8,10},{12,14},{1,3},{5,7},{9,11},{13,15},{16,18},{20,... | collective-permute-start | bytes 7864328 | tf_op jit(solution)/shard_map/ppermute | solution.py:31
  150.4 160.0 %collective-permute-start.6 = (bf16[2,256,2560]{1,2,0:T(8,128)(2,1)}, bf16[2,256,2560]{1,2,0:T(8,128)(2,1)S(1)}, u32[]{:S(2)}, u32[]{:S(2)}) collective-permute-start(bf16[2,256,2560]{1,2,0:T(8,128)(2,1)} %collective-permute-done.5), channel_id=1, source_target_pairs={{1,4},{5,8},{9,12},{13,0},{17,20},{21,24},{25,28},{29,16}} | collective-permute-start | bytes 7864328 | tf_op jit(solution)/shard_map/ppermute | solution.py:31
  151.7 158.7 %collective-permute-start.4 = (bf16[2,256,2560]{1,2,0:T(8,128)(2,1)}, bf16[2,256,2560]{1,2,0:T(8,128)(2,1)}, u32[]{:S(2)}, u32[]{:S(2)}) collective-permute-start(bf16[2,256,2560]{1,2,0:T(8,128)(2,1)} %collective-permute-done.3), channel_id=1, source_target_pairs={{2,0},{6,4},{10,8},{14,12},{18,16},{22,20},{26,24},{30,28}} | collective-permute-start | bytes 7864328 | tf_op jit(solution)/shard_map/ppermute | solution.py:31
  153.9 93.8 %collective-permute-start.10 = (bf16[5,1,52,384]{3,2,0,1:T(8,128)(2,1)}, bf16[5,1,52,384]{3,2,0,1:T(8,128)(2,1)}, u32[]{:S(2)}, u32[]{:S(2)}) collective-permute-start(bf16[5,1,52,384]{3,2,0,1:T(8,128)(2,1)} %pad_maximum_fusion.2), channel_id=1, source_target_pairs={{1,0},{2,1},{3,2},{4,3},{5,4},{6,5},{7,6},{8,7},{9,8},{10,9},{11,1... | collective-permute-start | bytes 599048 | tf_op jit(solution)/shard_map/ppermute | solution.py:25
  155.2 93.8 %collective-permute-start.9 = (bf16[5,1,52,384]{3,2,0,1:T(8,128)(2,1)}, bf16[5,1,52,384]{3,2,0,1:T(8,128)(2,1)}, u32[]{:S(2)}, u32[]{:S(2)}) collective-permute-start(bf16[5,1,52,384]{3,2,0,1:T(8,128)(2,1)} %pad_maximum_fusion.2), channel_id=1, source_target_pairs={{0,1},{1,2},{2,3},{3,4},{4,5},{5,6},{6,7},{7,8},{8,9},{9,10},{10,1... | collective-permute-start | bytes 599048 | tf_op jit(solution)/shard_map/ppermute | solution.py:22
  236.5 7.2 %copy-start.10 = (s32[16]{0:T(128)S(1)}, s32[16]{0:T(128)}, u32[]{:S(2)}) copy-start(s32[16]{0:T(128)} %param.14) | copy-start | bytes 196
  247.7 91.7 %collective-permute-start.8 = (bf16[2,256,2560]{1,2,0:T(8,128)(2,1)}, bf16[2,256,2560]{1,2,0:T(8,128)(2,1)S(1)}, u32[]{:S(2)}, u32[]{:S(2)}) collective-permute-start(bf16[2,256,2560]{1,2,0:T(8,128)(2,1)} %copy.56), channel_id=1, source_target_pairs={{1,4},{5,8},{9,12},{13,0},{17,20},{21,24},{25,28},{29,16}} | collective-permute-start | bytes 7864328 | tf_op jit(solution)/shard_map/ppermute | solution.py:31
  249.0 90.4 %collective-permute-start = (bf16[2,256,2560]{1,2,0:T(8,128)(2,1)}, bf16[2,256,2560]{1,2,0:T(8,128)(2,1)}, u32[]{:S(2)}, u32[]{:S(2)}) collective-permute-start(bf16[2,256,2560]{1,2,0:T(8,128)(2,1)} %copy.56), channel_id=1, source_target_pairs={{0,1},{4,5},{8,9},{12,13},{2,3},{6,7},{10,11},{14,15},{16,17},{20,... | collective-permute-start | bytes 7864328 | tf_op jit(solution)/shard_map/ppermute | solution.py:31
  310.4 13.1 %slice-start = ((s8[7962624]{0:T(1024)(128)(4,1)}), s8[4194304]{0:T(1024)(128)(4,1)S(1)}, s32[]{:S(2)}) async-start(s8[7962624]{0:T(1024)(128)(4,1)} %bitcast.134), calls=%async_computation.2 | async-start | bytes 8388608
  310.4 13.1 %slice-start.1 = ((s8[7962624]{0:T(1024)(128)(4,1)}), s8[3768320]{0:T(1024)(128)(4,1)S(1)}, s32[]{:S(2)}) async-start(s8[7962624]{0:T(1024)(128)(4,1)} %bitcast.134), calls=%async_computation.3 | async-start | bytes 7536640
  315.4 6.8 %copy-start.8 = (bf16[3,1,52,384]{3,2,1,0:T(8,128)(2,1)S(1)}, bf16[3,1,52,384]{3,2,1,0:T(8,128)(2,1)}, u32[]{:S(2)}) copy-start(bf16[3,1,52,384]{3,2,1,0:T(8,128)(2,1)} %param.15) | copy-start | bytes 359428
  315.4 25.6 %collective-permute-start.7 = (bf16[2,2,256,2560]{2,3,1,0:T(8,128)(2,1)}, bf16[2,2,256,2560]{2,3,1,0:T(8,128)(2,1)S(1)}, u32[]{:S(2)}, u32[]{:S(2)}) collective-permute-start(bf16[2,2,256,2560]{2,3,1,0:T(8,128)(2,1)} %pad_maximum_fusion.1), channel_id=1, source_target_pairs={{0,1},{4,5},{8,9},{12,13},{16,17},{20,21},{24,25},{28,29}} | collective-permute-start | bytes 15728648 | tf_op jit(solution)/shard_map/ppermute | solution.py:31
  317.2 6.3 %copy-start.12 = (f32[384]{0:T(512)S(1)}, f32[384]{0:T(512)}, u32[]{:S(2)}) copy-start(f32[384]{0:T(512)} %param.19) | copy-start | bytes 4612
  320.3 19.1 %collective-permute-start.2 = (bf16[2,256,2560]{1,2,0:T(8,128)(2,1)}, bf16[2,256,2560]{1,2,0:T(8,128)(2,1)S(1)}, u32[]{:S(2)}, u32[]{:S(2)}) collective-permute-start(bf16[2,256,2560]{1,2,0:T(8,128)(2,1)} %collective-permute-done.1), channel_id=1, source_target_pairs={{3,2},{7,6},{11,10},{15,14},{2,3},{6,7},{10,11},{14,15},{19,18},{2... | collective-permute-start | bytes 7864328 | tf_op jit(solution)/shard_map/ppermute | solution.py:31
  354.3 7.1 %copy-start = (f32[10,1024,256]{2,1,0:T(8,128)}, f32[10,1024,256]{2,1,0:T(8,128)S(1)}, u32[]{:S(2)}) copy-start(f32[10,1024,256]{2,1,0:T(8,128)S(1)} %fusion.56) | copy-start | bytes 31457284
  354.3 7.1 %copy-start.4 = (bf16[256,2560]{1,0:T(8,128)(2,1)S(1)}, bf16[256,2560]{1,0:T(8,128)(2,1)}, u32[]{:S(2)}) copy-start(bf16[256,2560]{1,0:T(8,128)(2,1)} %reduce_sum.69) | copy-start | bytes 3932164
  (5 other events, 12.8 us)
Sparse Core Ops, SparseCore 0:
  11.4 111.5 all-gather.3
  136.6 170.6 all-gather.5
